TPU v7x, 512 devices: a whole 4x4x16 slice. The times are simulated.
512 devices in a mesh: seq: 32 (over z, core), tensor: 16 (over y, x).
Axes of the slice: x: 4, y: 4, z: 16, core: 2. Of those that a mesh axis runs over, the one named last changes fastest.
Arguments:
- hidden: bfloat16 [4, 64, 5120], P(None, None, 'seq'), may hold values from -400 to 400
- norm_gain: bfloat16 [5120], P('seq'), may hold values from 0.099609375 to 1.8984375
- w_qkv: bfloat16 [5120, 7168], P('seq', 'tensor'), may hold values from -0.078125 to 0.078125
- b_qkv: bfloat16 [7168], P('tensor'), may hold values from -3 to 3
- w_out: bfloat16 [5120, 5120], P('tensor', 'seq'), may hold values from -0.078125 to 0.078125
- prefix_key_cache: bfloat16 [16, 12288, 1024], P('tensor', 'seq'), may hold values from -140 to 140
- prefix_value_cache: bfloat16 [16, 12288, 1024], P('tensor', 'seq'), may hold values from -6 to 6
- suffix_key_cache: bfloat16 [64, 4096, 1024], P('tensor', 'seq'), may hold values from -8 to 8
- suffix_value_cache: bfloat16 [64, 4096, 1024], P('tensor', 'seq'), may hold values from -6 to 6
- prefix_lens: int32 [16], P('tensor'), may hold values from 1 to 12288, as said below
- suffix_lens: int32 [64], P('tensor'), may hold values from 0 to 4096, as said below
Outputs:
- attn_out: float32 [4, 64, 5120], P(None, 'tensor', 'seq')
- new_keys: float32 [64, 4, 1024], P('tensor')
- new_values: float32 [64, 4, 1024], P('tensor')
Inputs may be any that keep to these rules, and one draw needn't show every extreme that they name: `prefix_lens`: some group has exactly 12288 live slots and some exactly one. `suffix_lens`: some request has exactly 4096 live slots and some none.
All inputs are finite; a program needn't handle non-finite values.
Results may differ from a plain program's by a relative error of at most 0.012.
The roundings to bfloat16 on the way count: a program that leaves them out, or rounds other values in their place, can miss the bound.
Values may be sent and summed in bfloat16 or wider, within the bound.
No kernel may reach another device: no remote copies, remote signals or barrier semaphores. Data moves between devices by JAX's collectives and lax.ppermute only.
A program may use at most 64 MiB of HBM per device.

v0:
```python
import jax
import jax.numpy as jnp
from jax import lax
from jax.sharding import PartitionSpec as P

D = 5120
QUERY_HEADS = 40
KEY_HEADS = 8
HEAD_SIZE = 128
KEY_COLUMNS = 1024
epsilon = 1e-06
masked_fill = -1e30


def apply_rotary(values, token_positions):
    half = values.shape[-1] // 2
    freq = jnp.exp(
        -(jnp.arange(half, dtype=jnp.float32) * (2.0 / values.shape[-1]))
        * jnp.log(jnp.float32(1000000.0))
    )
    angles = token_positions[..., None, None] * freq
    cosine = jnp.cos(angles)
    sine = jnp.sin(angles)
    left = values[..., :half]
    right = values[..., half:]
    return jnp.concatenate([left * cosine - right * sine, right * cosine + left * sine], axis=-1)


def body(
    hidden,
    norm_gain,
    w_qkv,
    b_qkv,
    w_out,
    prefix_key_cache,
    prefix_value_cache,
    suffix_key_cache,
    suffix_value_cache,
    prefix_lens,
    suffix_lens,
):
    decode_step_count = hidden.shape[0]
    request_count = suffix_lens.shape[0]
    prefix_count = prefix_key_cache.shape[1]
    suffix_count = suffix_key_cache.shape[1]
    query_group_width = QUERY_HEADS // KEY_HEADS
    query_width = QUERY_HEADS * HEAD_SIZE
    query_rows = decode_step_count * query_group_width
    scale = float(HEAD_SIZE) ** (-0.5)
    seq_index = lax.axis_index("seq")
    xf = hidden.astype(jnp.float32)
    squares = lax.psum(jnp.sum(xf * xf, axis=2), "seq")
    normed = (
        xf * lax.rsqrt(squares / D + epsilon)[..., None] * norm_gain.astype(jnp.float32)
    ).astype(jnp.bfloat16)
    partial_value = jnp.einsum("sbd,dc->sbc", normed, w_qkv, preferred_element_type=jnp.float32)
    bias = b_qkv.astype(jnp.float32)
    summed_cols = lax.psum(partial_value, "seq") + bias
    combined_output = lax.all_to_all(summed_cols, "tensor", split_axis=1, concat_axis=2, tiled=True)
    token_positions = (
        (prefix_lens[0] + suffix_lens)[None, :]
        + jnp.arange(decode_step_count, dtype=jnp.int32)[:, None]
    ).astype(jnp.float32)
    query_matrix = apply_rotary(
        combined_output[..., :query_width].reshape(
            decode_step_count, request_count, QUERY_HEADS, HEAD_SIZE
        ),
        token_positions,
    ).astype(jnp.bfloat16)
    keys_float = apply_rotary(
        combined_output[..., query_width : query_width + KEY_COLUMNS].reshape(
            decode_step_count, request_count, KEY_HEADS, HEAD_SIZE
        ),
        token_positions,
    )
    values_float = combined_output[..., query_width + KEY_COLUMNS :].reshape(
        decode_step_count, request_count, KEY_HEADS, HEAD_SIZE
    )
    current_keys = keys_float.astype(jnp.bfloat16)
    current_values = values_float.astype(jnp.bfloat16)
    new_keys = keys_float.reshape(decode_step_count, request_count, KEY_COLUMNS).transpose(1, 0, 2)
    new_values = values_float.reshape(decode_step_count, request_count, KEY_COLUMNS).transpose(
        1, 0, 2
    )
    query_by_group = (
        query_matrix.reshape(
            decode_step_count, request_count, KEY_HEADS, query_group_width, HEAD_SIZE
        )
        .transpose(1, 2, 0, 3, 4)
        .reshape(request_count, KEY_HEADS, query_rows, HEAD_SIZE)
    )
    prefix_key_block = prefix_key_cache[0].reshape(prefix_count, KEY_HEADS, HEAD_SIZE)
    prefix_value_block = prefix_value_cache[0].reshape(prefix_count, KEY_HEADS, HEAD_SIZE)
    suffix_key_block = suffix_key_cache.reshape(request_count, suffix_count, KEY_HEADS, HEAD_SIZE)
    suffix_value_block = suffix_value_cache.reshape(
        request_count, suffix_count, KEY_HEADS, HEAD_SIZE
    )
    score_pre = (
        jnp.einsum(
            "rhqd,phd->rhqp", query_by_group, prefix_key_block, preferred_element_type=jnp.float32
        )
        * scale
    )
    score_suf = (
        jnp.einsum(
            "rhqd,rshd->rhqs", query_by_group, suffix_key_block, preferred_element_type=jnp.float32
        )
        * scale
    )
    pre_mask = (
        seq_index * prefix_count + jnp.arange(prefix_count, dtype=jnp.int32) < prefix_lens[0]
    )[None, None, None, :]
    suf_mask = (
        (seq_index * suffix_count + jnp.arange(suffix_count, dtype=jnp.int32))[None, :]
        < suffix_lens[:, None]
    )[:, None, None, :]
    fill_pre = jnp.where(pre_mask, score_pre, masked_fill)
    fill_suf = jnp.where(suf_mask, score_suf, masked_fill)
    local_max = jnp.maximum(jnp.max(fill_pre, axis=3), jnp.max(fill_suf, axis=3))
    prob_pre = jnp.where(pre_mask, jnp.exp(fill_pre - local_max[..., None]), 0.0)
    prob_suf = jnp.where(suf_mask, jnp.exp(fill_suf - local_max[..., None]), 0.0)
    local_weight = jnp.sum(prob_pre, axis=3) + jnp.sum(prob_suf, axis=3)
    local_acc = jnp.einsum(
        "rhqp,phd->rhqd",
        prob_pre.astype(jnp.bfloat16),
        prefix_value_block,
        preferred_element_type=jnp.float32,
    )
    local_acc = local_acc + jnp.einsum(
        "rhqs,rshd->rhqd",
        prob_suf.astype(jnp.bfloat16),
        suffix_value_block,
        preferred_element_type=jnp.float32,
    )
    global_max = lax.pmax(local_max, "seq")
    factor = jnp.exp(local_max - global_max)
    global_weight, global_acc = lax.psum(
        (local_weight * factor, local_acc * factor[..., None]), "seq"
    )
    fresh_k = current_keys.transpose(1, 2, 0, 3)
    fresh_v = current_values.transpose(1, 2, 0, 3)
    score_new = (
        jnp.einsum("rhqd,rhid->rhqi", query_by_group, fresh_k, preferred_element_type=jnp.float32)
        * scale
    )
    new_mask = (
        (jnp.arange(query_rows, dtype=jnp.int32) // query_group_width)[:, None]
        >= jnp.arange(decode_step_count, dtype=jnp.int32)[None, :]
    )[None, None]
    fill_new = jnp.where(new_mask, score_new, masked_fill)
    new_max = jnp.max(fill_new, axis=3)
    prob_new = jnp.where(new_mask, jnp.exp(fill_new - new_max[..., None]), 0.0)
    top = jnp.maximum(global_max, new_max)
    factor_old = jnp.exp(global_max - top)
    factor_new = jnp.exp(new_max - top)
    total = global_weight * factor_old + jnp.sum(prob_new, axis=3) * factor_new
    new_acc = jnp.einsum(
        "rhqi,rhid->rhqd",
        prob_new.astype(jnp.bfloat16),
        fresh_v,
        preferred_element_type=jnp.float32,
    )
    summed = global_acc * factor_old[..., None] + new_acc * factor_new[..., None]
    attention_output = (summed / total[..., None]).astype(jnp.bfloat16)
    heads_local = (
        attention_output.reshape(
            request_count, KEY_HEADS, decode_step_count, query_group_width, HEAD_SIZE
        )
        .transpose(2, 0, 1, 3, 4)
        .reshape(decode_step_count, request_count, query_width)
    )
    by_heads = lax.all_to_all(heads_local, "tensor", split_axis=2, concat_axis=1, tiled=True)
    projected = jnp.einsum("sbc,cd->sbd", by_heads, w_out, preferred_element_type=jnp.float32)
    owned = lax.psum_scatter(projected, "tensor", scatter_dimension=1, tiled=True)
    return (owned, new_keys, new_values)


def solution(mesh):
    placed = (
        P(None, None, "seq"),
        P("seq"),
        P("seq", "tensor"),
        P("tensor"),
        P("tensor", "seq"),
        P("tensor", "seq", None),
        P("tensor", "seq", None),
        P("tensor", "seq", None),
        P("tensor", "seq", None),
        P("tensor"),
        P("tensor"),
    )
    return jax.shard_map(
        body,
        mesh=mesh,
        in_specs=placed,
        out_specs=(P(None, "tensor", "seq"), P("tensor", None, None), P("tensor", None, None)),
        check_vma=False,
    )
```

profile of v0, /device:TPU:2, one launch (start us, length us, event | category | flops | bytes accessed | tf_op | source)
XLA Modules:
  0.0 850.0 jit_solution(4505224170774639408)
XLA Ops:
  7.2 0.0 copy-start
  7.2 0.0 copy-start.19
  7.2 0.0 copy-start.16
  7.2 0.0 all-reduce.5.cloned.1.call-start
  7.3 0.8 convert_element_type.43
  8.0 1.0 fusion.22
  9.1 54.7 %psum.28 = f32[4,64]{1,0:T(4,128)S(1)} all-reduce(f32[4,64]{1,0:T(4,128)S(1)} %fusion.22), channel_id=1, replica_groups=mesh['seq'=32,'tensor'=16] {'seq'}, use_global_device_ids=true, to_apply=%region_1.0 | all-reduce | flops 256 | bytes 2048 | tf_op jit(solution)/shard_map/psum | solution.py:52
  63.8 2.1 fusion.29
  65.9 0.0 all-reduce.5.cloned.1.call-update
  66.6 0.1 add_convert_fusion.1
  66.6 0.1 multiply_cosine_fusion
  66.9 0.0 copy-done.4
  66.9 0.2 copy.148
  67.1 2.2 copy.149
  69.3 0.0 copy-done.13
  69.3 199.9 %all-reduce.5.cloned.1.call-done = f32[4,64,448]{2,1,0:T(8,128)} async-done(((f32[4,64,448]{2,1,0:T(8,128)}), f32[4,64,448]{2,1,0:T(8,128)}) %all-reduce.5.cloned.1.call-update) | async-done | bytes 458768 | tf_op jit(solution)/shard_map/psum | solution.py:58
  269.2 1.1 broadcast_add_fusion
  270.4 1.1 copy.98
  271.5 7.3 all-to-all-start
  278.8 0.0 all-reduce.7.cloned.1.call-start
  278.8 0.5 iota_compare_fusion
  279.4 0.1 broadcast_compare_fusion
  279.4 9.8 %all-to-all-done = f32[4,64,448]{2,0,1:T(4,128)S(1)} async-done(((f32[4,64,448]{2,0,1:T(4,128)}), f32[4,64,448]{2,0,1:T(4,128)S(1)}, u32[]{:S(2)}, u32[]{:S(2)}) %all-to-all-start) | async-done | bytes 458784 | tf_op jit(solution)/shard_map/all_to_all | solution.py:59
  289.2 0.3 copy.99
  289.5 0.3 all_to_all.29
  289.9 0.6 slice_bitcast_fusion.1
  290.6 0.1 reshape.150
  290.7 0.2 fusion.51
  290.9 0.4 subtract_convert_fusion
  291.3 0.2 maximum_bitcast_fusion
  291.6 1.4 fusion.52
  293.0 0.7 fusion.53
  293.7 0.0 copy-done.2
  293.7 91.2 %pmax.7 = f32[4,8,20]{2,1,0:T(8,128)} all-reduce(f32[4,8,20]{2,1,0:T(8,128)S(1)} %copy_maximum_fusion), channel_id=1, replica_groups=mesh['seq'=32,'tensor'=16] {'seq'}, use_global_device_ids=true, to_apply=%region_5.6 | all-reduce | flops 640 | bytes 5120 | tf_op jit(solution)/shard_map/pmax | solution.py:135
  384.9 1.5 multiply_subtract_fusion
  386.4 1.9 fusion.20
  388.2 1.1 fusion.12
  389.3 90.0 %psum.31 = f32[4,8,20]{2,1,0:T(8,128)S(1)} all-reduce(f32[4,8,20]{2,1,0:T(8,128)S(1)} %get-tuple-element.6), channel_id=1, replica_groups=mesh['seq'=32,'tensor'=16] {'seq'}, use_global_device_ids=true, to_apply=%region_10.11 | all-reduce | flops 640 | bytes 5120 | tf_op jit(solution)/shard_map/psum | solution.py:137
  479.4 1.3 convolution_bitcast_fusion
  480.7 0.0 copy-done.1
  480.7 0.0 copy-done.6
  480.7 0.0 copy-start.3
  480.7 0.0 copy-start.7
  480.8 1.2 fusion.4
  481.9 0.0 all-reduce.7.cloned.1.call-update
  481.9 0.0 all-reduce.9.cloned.1.call-start
  482.0 0.3 fusion.54
  482.3 0.1 fusion.37
  482.5 198.4 %all-reduce.7.cloned.1.call-done = f32[4,8,20,128]{3,2,0,1:T(8,128)} async-done(((f32[4,8,20,128]{3,2,0,1:T(8,128)}), f32[4,8,20,128]{3,2,0,1:T(8,128)}) %all-reduce.7.cloned.1.call-update) | async-done | bytes 327696 | tf_op jit(solution)/shard_map/psum | solution.py:137
  680.9 1.5 fusion.6
  682.3 0.1 copy.121
  682.4 4.5 copy.139
  686.9 11.0 %reshape.165 = bf16[16,2,2560]{2,1,0:T(2,128)(2,1)S(1)} reshape(bf16[5120,4,4]{2,1,0:T(4,128)(2,1)} %bitcast.84) | data formatting | bytes 327680
  697.9 13.9 %all_to_all.36 = bf16[16,2,2560]{2,1,0:T(2,128)(2,1)S(1)} all-to-all(bf16[16,2,2560]{2,1,0:T(2,128)(2,1)S(1)} %reshape.165), channel_id=1, replica_groups=mesh['seq'=32,'tensor'=16] {'tensor'}, dimensions={0} | all-to-all | bytes 327680 | tf_op jit(solution)/shard_map/all_to_all | solution.py:172
  711.8 12.3 %reshape.166 = bf16[5120,4,4]{2,1,0:T(4,128)(2,1)} reshape(bf16[16,2,2560]{2,1,0:T(2,128)(2,1)S(1)} %all_to_all.36) | data formatting | bytes 327680
  724.1 6.4 copy.140
  730.5 0.1 copy.125
  730.6 0.1 all_to_all.33
  730.7 0.9 fusion.34
  731.7 0.0 all-reduce.9.cloned.1.call-update
  731.7 1.3 dynamic-slice
  733.6 0.7 fusion.46
  734.4 107.7 %all-reduce.9.cloned.1.call-done = f32[4,64,160]{2,1,0:T(8,128)} async-done(((f32[4,64,160]{2,1,0:T(8,128)}), f32[4,64,160]{2,1,0:T(8,128)}) %all-reduce.9.cloned.1.call-update) | async-done | bytes 163856
  842.1 1.4 constant_dynamic-slice_fusion
  (49 shorter events, 0.2 us)
Async XLA Ops:
  7.2 284.4 %copy-start = (bf16[4,128,1024]{2,1,0:T(8,128)(2,1)S(1)}, bf16[4,128,1024]{2,1,0:T(8,128)(2,1)}, u32[]{:S(2)}) copy-start(bf16[4,128,1024]{2,1,0:T(8,128)(2,1)} %param.18) | copy-start | bytes 3145732
  7.2 59.4 %copy-start.19 = (s32[4]{0:T(128)S(1)}, s32[4]{0:T(128)}, u32[]{:S(2)}) copy-start(s32[4]{0:T(128)} %param.21) | copy-start | bytes 52
  7.2 59.6 %copy-start.16 = (bf16[448]{0:T(512)(128)(2,1)S(1)}, bf16[448]{0:T(512)(128)(2,1)}, u32[]{:S(2)}) copy-start(bf16[448]{0:T(512)(128)(2,1)} %param.14) | copy-start | bytes 2692
  7.2 59.7 %copy-start.4 = (bf16[1,384,1024]{2,1,0:T(8,128)(2,1)S(1)}, bf16[1,384,1024]{2,1,0:T(8,128)(2,1)}, u32[]{:S(2)}) copy-start(bf16[1,384,1024]{2,1,0:T(8,128)(2,1)} %param.16) | copy-start | bytes 2359300
  7.2 262.0 %all-reduce.5.cloned.1.call-start = ((), (), s32[]{:S(2)}) async-start(), calls=%async_computation.2 | async-start | bytes 1048576 | tf_op jit(solution)/shard_map/psum | solution.py:58
  66.8 2.5 copy-start.12
  66.8 2.5 copy-start.13
  69.3 223.7 %copy-start.15 = (pred[384]{0:T(512)(128)(4,1)}, pred[384]{0:T(512)(128)(4,1)S(1)}, u32[]{:S(2)}) copy-start(pred[384]{0:T(512)(128)(4,1)S(1)} %add_compare_fusion) | copy-start | bytes 1156
  271.5 17.7 %all-to-all-start = ((f32[4,64,448]{2,0,1:T(4,128)}), f32[4,64,448]{2,0,1:T(4,128)S(1)}, u32[]{:S(2)}, u32[]{:S(2)}) async-start(f32[4,64,448]{2,0,1:T(4,128)} %copy.98), calls=%async_computation | async-start | bytes 1048576 | tf_op jit(solution)/shard_map/all_to_all | solution.py:59
  278.8 402.1 %all-reduce.7.cloned.1.call-start = ((), (), s32[]{:S(2)}) async-start(), calls=%async_computation.3 | async-start | bytes 786432 | tf_op jit(solution)/shard_map/psum | solution.py:137
  279.4 12.2 %copy-start.18 = (pred[4,128]{1,0:T(4,128)(4,1)}, pred[4,128]{1,0:T(4,128)(4,1)S(1)}, u32[]{:S(2)}) copy-start(pred[4,128]{1,0:T(4,128)(4,1)S(1)} %broadcast_compare_fusion) | copy-start | bytes 1540
  291.6 2.1 copy-start.2
  293.7 185.6 %copy-start.5 = (bf16[48,8,8,128]{3,2,1,0:T(8,128)(2,1)S(1)}, bf16[48,8,8,128]{3,2,1,0:T(8,128)(2,1)}, u32[]{:S(2)}) copy-start(bf16[48,8,8,128]{3,2,1,0:T(8,128)(2,1)} %copy.149) | copy-start | bytes 2359300
  384.9 4.4 copy-start.9
  384.9 4.4 copy-start.14
  479.4 1.3 copy-start.1
  479.4 1.3 copy-start.6
  480.7 1.3 copy-start.3
  480.7 1.3 copy-start.7
  480.7 1.3 copy-start.8
  480.7 1.3 copy-start.17
  480.7 1.7 copy-start.10
  481.9 360.1 %all-reduce.9.cloned.1.call-start = ((), (), s32[]{:S(2)}) async-start(), calls=%async_computation.4 | async-start | bytes 524288
  724.1 6.6 copy-start.11
Sparse Core Ops, SparseCore 0:
  66.0 203.1 all-reduce.4
  482.1 198.7 all-reduce.6
  731.8 110.2 all-reduce.8
where the time goes:
time: 851 us; the launch traced here: 850 us
  waiting for transfers between devices  516 us (61%)
  blocking collectives  250 us (29%)
  local copies, waits for them, and re-layouts  42.4 us (5%)
  between operations  15.5 us (2%)
  other arithmetic  9.67 us (1%)
  matrix products  9.33 us (1%)
    psum x1, waiting for transfers between devices, body(): summed_cols = lax.psum(partial_value, 'seq') + bias  200 us
    psum x1, waiting for transfers between devices, body(): lax.psum((local_weight * factor, local_acc * factor[..., None]), 'seq')  198 us
    unnamed x4, waiting for transfers between devices  108 us
    pmax x1, blocking collectives, body(): global_max = lax.pmax(local_max, 'seq')  91.2 us
    psum x1, blocking collectives, body(): lax.psum((local_weight * factor, local_acc * factor[..., None]), 'seq')  90 us
    psum x1, blocking collectives, body(): squares = lax.psum(jnp.sum(xf * xf, axis=2), 'seq')  54.7 us
    unnamed x46, local copies, waits for them, and re-layouts  28.4 us
  transfers between devices with their start and end apart: 4, of which 4 were waited for; matrix products, arithmetic and copies ran while one was open for 1% of the time, Pallas kernels for 0%

commit v1 on v0

--- a/solution.py
+++ b/solution.py
@@ -169,7 +169,11 @@
         .transpose(2, 0, 1, 3, 4)
         .reshape(decode_step_count, request_count, query_width)
     )
-    by_heads = lax.all_to_all(heads_local, "tensor", split_axis=2, concat_axis=1, tiled=True)
+    all_values = lax.axis_size("tensor")
+    f_now = jnp.split(heads_local, all_values, 2)
+    everything = jnp.stack(f_now)
+    earlier = lax.all_to_all(everything, axis_name="tensor", split_axis=0, concat_axis=0)
+    by_heads = jnp.concatenate(earlier, 1)
     projected = jnp.einsum("sbc,cd->sbd", by_heads, w_out, preferred_element_type=jnp.float32)
     owned = lax.psum_scatter(projected, "tensor", scatter_dimension=1, tiled=True)
     return (owned, new_keys, new_values)

time: 851 us -> 818 us (0.961)
  local copies, waits for them, and re-layouts: 42.4 us -> 9.09 us
    unnamed x46 -> x59, local copies, waits for them, and re-layouts: 28.4 us -> 5.82 us
where the time goes in v1:
time: 818 us; the launch traced here: 817 us
  waiting for transfers between devices  516 us (63%)
  blocking collectives  250 us (31%)
  between operations  15.6 us (2%)
  other arithmetic  9.67 us (1%)
  matrix products  9.33 us (1%)
  local copies, waits for them, and re-layouts  9.09 us (1%)
    psum x1, waiting for transfers between devices, body(): summed_cols = lax.psum(partial_value, 'seq') + bias  200 us
    psum x1, waiting for transfers between devices, body(): lax.psum((local_weight * factor, local_acc * factor[..., None]), 'seq')  198 us
    unnamed x4, waiting for transfers between devices  108 us
    pmax x1, blocking collectives, body(): global_max = lax.pmax(local_max, 'seq')  91.2 us
    psum x1, blocking collectives, body(): lax.psum((local_weight * factor, local_acc * factor[..., None]), 'seq')  90 us
    psum x1, blocking collectives, body(): squares = lax.psum(jnp.sum(xf * xf, axis=2), 'seq')  54.7 us
  transfers between devices with their start and end apart: 4, of which 4 were waited for; matrix products, arithmetic and copies ran while one was open for 1% of the time, Pallas kernels for 0%

profile of v1, /device:TPU:2, one launch (start us, length us, event | category | flops | bytes accessed | tf_op | source)
XLA Modules:
  0.0 816.9 jit_solution(3058243633366432471)
XLA Ops:
  7.2 0.0 copy-start
  7.2 0.0 all-reduce.5.cloned.1.call-start
  7.3 0.8 convert_element_type.43
  8.0 1.0 fusion.22
  9.1 54.7 %psum.28 = f32[4,64]{1,0:T(4,128)S(1)} all-reduce(f32[4,64]{1,0:T(4,128)S(1)} %fusion.22), channel_id=1, replica_groups=mesh['seq'=32,'tensor'=16] {'seq'}, use_global_device_ids=true, to_apply=%region_1.0 | all-reduce | flops 256 | bytes 2048 | tf_op jit(solution)/shard_map/psum | solution.py:52
  63.8 2.1 fusion.29
  65.9 0.0 all-reduce.5.cloned.1.call-update
  66.6 0.0 copy-done.19
  66.6 0.1 add_convert_fusion.1
  66.6 0.1 multiply_cosine_fusion
  66.9 0.2 copy.154
  67.1 2.2 copy.155
  69.3 199.9 %all-reduce.5.cloned.1.call-done = f32[4,64,448]{2,1,0:T(8,128)} async-done(((f32[4,64,448]{2,1,0:T(8,128)}), f32[4,64,448]{2,1,0:T(8,128)}) %all-reduce.5.cloned.1.call-update) | async-done | bytes 458768 | tf_op jit(solution)/shard_map/psum | solution.py:58
  269.2 1.1 broadcast_add_fusion
  270.4 1.1 copy.109
  271.5 7.3 all-to-all-start
  278.8 0.0 all-reduce.7.cloned.1.call-start
  278.8 0.5 iota_compare_fusion
  279.4 0.1 broadcast_compare_fusion
  279.4 9.8 %all-to-all-done = f32[4,64,448]{2,0,1:T(4,128)S(1)} async-done(((f32[4,64,448]{2,0,1:T(4,128)}), f32[4,64,448]{2,0,1:T(4,128)S(1)}, u32[]{:S(2)}, u32[]{:S(2)}) %all-to-all-start) | async-done | bytes 458784 | tf_op jit(solution)/shard_map/all_to_all | solution.py:59
  289.2 0.3 copy.110
  289.6 0.3 all_to_all.19
  289.9 0.6 slice_bitcast_fusion.1
  290.6 0.1 reshape.156
  290.7 0.2 fusion.51
  290.9 0.4 subtract_convert_fusion
  291.3 0.2 maximum_bitcast_fusion
  291.6 1.4 fusion.52
  293.0 0.7 fusion.53
  293.7 91.2 %pmax.7 = f32[4,8,20]{2,1,0:T(8,128)} all-reduce(f32[4,8,20]{2,1,0:T(8,128)S(1)} %copy_maximum_fusion), channel_id=1, replica_groups=mesh['seq'=32,'tensor'=16] {'seq'}, use_global_device_ids=true, to_apply=%region_5.6 | all-reduce | flops 640 | bytes 5120 | tf_op jit(solution)/shard_map/pmax | solution.py:135
  384.9 1.5 multiply_subtract_fusion
  386.4 1.9 fusion.20
  388.2 1.1 fusion.12
  389.3 90.0 %psum.31 = f32[4,8,20]{2,1,0:T(8,128)S(1)} all-reduce(f32[4,8,20]{2,1,0:T(8,128)S(1)} %get-tuple-element.6), channel_id=1, replica_groups=mesh['seq'=32,'tensor'=16] {'seq'}, use_global_device_ids=true, to_apply=%region_10.11 | all-reduce | flops 640 | bytes 5120 | tf_op jit(solution)/shard_map/psum | solution.py:137
  479.4 1.3 convolution_bitcast_fusion
  480.7 0.0 copy-start.7
  480.8 1.2 fusion.4
  481.9 0.0 all-reduce.7.cloned.1.call-update
  481.9 0.0 all-reduce.9.cloned.1.call-start
  482.0 0.3 fusion.54
  482.3 0.1 fusion.37
  482.5 198.4 %all-reduce.7.cloned.1.call-done = f32[4,8,20,128]{3,2,0,1:T(8,128)} async-done(((f32[4,8,20,128]{3,2,0,1:T(8,128)}), f32[4,8,20,128]{3,2,0,1:T(8,128)}) %all-reduce.7.cloned.1.call-update) | async-done | bytes 327696 | tf_op jit(solution)/shard_map/psum | solution.py:137
  680.9 1.5 fusion.6
  682.4 0.1 copy.132
  682.4 0.0 copy-start.11
  682.4 0.1 copy.133
  682.5 0.1 reshape.162
  682.6 0.1 constant_dynamic-update-slice_fusion.14
  682.7 0.1 constant_dynamic-update-slice_fusion.12
  682.8 0.1 constant_dynamic-update-slice_fusion.10
  683.0 0.1 constant_dynamic-update-slice_fusion.8
  683.1 0.1 constant_dynamic-update-slice_fusion.6
  683.2 0.1 constant_dynamic-update-slice_fusion.4
  683.3 0.1 constant_dynamic-update-slice_fusion.2
  683.4 0.1 constant_dynamic-update-slice_fusion
  683.5 14.0 %all_to_all.23 = bf16[16,4,4,320]{3,2,1,0:T(4,128)(2,1)S(1)} all-to-all(bf16[16,4,4,320]{3,2,1,0:T(4,128)(2,1)S(1)} %constant_dynamic-update-slice_fusion), channel_id=1, replica_groups=mesh['seq'=32,'tensor'=16] {'tensor'}, dimensions={0} | all-to-all | bytes 327680 | tf_op jit(solution)/shard_map/all_to_all | solution.py:175
  697.5 0.1 copy.134
  697.6 0.1 reshape.164
  697.7 0.9 fusion.34
  698.6 0.0 all-reduce.9.cloned.1.call-update
  698.7 1.3 dynamic-slice
  700.6 0.7 fusion.46
  701.3 107.7 %all-reduce.9.cloned.1.call-done = f32[4,64,160]{2,1,0:T(8,128)} async-done(((f32[4,64,160]{2,1,0:T(8,128)}), f32[4,64,160]{2,1,0:T(8,128)}) %all-reduce.9.cloned.1.call-update) | async-done | bytes 163856
  809.0 1.4 constant_dynamic-slice_fusion
  (63 shorter events, 0.3 us)
Async XLA Ops:
  7.2 284.4 %copy-start = (bf16[4,128,1024]{2,1,0:T(8,128)(2,1)S(1)}, bf16[4,128,1024]{2,1,0:T(8,128)(2,1)}, u32[]{:S(2)}) copy-start(bf16[4,128,1024]{2,1,0:T(8,128)(2,1)} %param.18) | copy-start | bytes 3145732
  7.2 59.4 %copy-start.19 = (s32[4]{0:T(128)S(1)}, s32[4]{0:T(128)}, u32[]{:S(2)}) copy-start(s32[4]{0:T(128)} %param.21) | copy-start | bytes 52
  7.2 59.6 %copy-start.16 = (bf16[448]{0:T(512)(128)(2,1)S(1)}, bf16[448]{0:T(512)(128)(2,1)}, u32[]{:S(2)}) copy-start(bf16[448]{0:T(512)(128)(2,1)} %param.14) | copy-start | bytes 2692
  7.2 59.7 %copy-start.4 = (bf16[1,384,1024]{2,1,0:T(8,128)(2,1)S(1)}, bf16[1,384,1024]{2,1,0:T(8,128)(2,1)}, u32[]{:S(2)}) copy-start(bf16[1,384,1024]{2,1,0:T(8,128)(2,1)} %param.16) | copy-start | bytes 2359300
  7.2 262.0 %all-reduce.5.cloned.1.call-start = ((), (), s32[]{:S(2)}) async-start(), calls=%async_computation.2 | async-start | bytes 1048576 | tf_op jit(solution)/shard_map/psum | solution.py:58
  66.8 2.5 copy-start.13
  66.8 222.4 %copy-start.12 = (f32[4,4,64]{2,0,1:T(4,128)}, f32[4,4,64]{2,0,1:T(4,128)S(1)}, u32[]{:S(2)}) copy-start(f32[4,4,64]{2,0,1:T(4,128)S(1)} %get-tuple-element.20) | copy-start | bytes 12292
  69.3 223.7 %copy-start.15 = (pred[384]{0:T(512)(128)(4,1)}, pred[384]{0:T(512)(128)(4,1)S(1)}, u32[]{:S(2)}) copy-start(pred[384]{0:T(512)(128)(4,1)S(1)} %add_compare_fusion) | copy-start | bytes 1156
  271.5 17.7 %all-to-all-start = ((f32[4,64,448]{2,0,1:T(4,128)}), f32[4,64,448]{2,0,1:T(4,128)S(1)}, u32[]{:S(2)}, u32[]{:S(2)}) async-start(f32[4,64,448]{2,0,1:T(4,128)} %copy.109), calls=%async_computation | async-start | bytes 1048576 | tf_op jit(solution)/shard_map/all_to_all | solution.py:59
  278.8 402.1 %all-reduce.7.cloned.1.call-start = ((), (), s32[]{:S(2)}) async-start(), calls=%async_computation.3 | async-start | bytes 786432 | tf_op jit(solution)/shard_map/psum | solution.py:137
  279.4 12.2 %copy-start.18 = (pred[4,128]{1,0:T(4,128)(4,1)}, pred[4,128]{1,0:T(4,128)(4,1)S(1)}, u32[]{:S(2)}) copy-start(pred[4,128]{1,0:T(4,128)(4,1)S(1)} %broadcast_compare_fusion) | copy-start | bytes 1540
  291.6 2.1 copy-start.2
  293.7 185.6 %copy-start.5 = (bf16[48,8,8,128]{3,2,1,0:T(8,128)(2,1)S(1)}, bf16[48,8,8,128]{3,2,1,0:T(8,128)(2,1)}, u32[]{:S(2)}) copy-start(bf16[48,8,8,128]{3,2,1,0:T(8,128)(2,1)} %copy.155) | copy-start | bytes 2359300
  384.9 4.4 copy-start.9
  384.9 4.4 copy-start.14
  479.4 1.3 copy-start.1
  479.4 1.3 copy-start.6
  480.7 1.3 copy-start.3
  480.7 1.3 copy-start.7
  480.7 1.3 copy-start.8
  480.7 1.3 copy-start.17
  480.8 1.7 copy-start.10
  481.9 327.1 %all-reduce.9.cloned.1.call-start = ((), (), s32[]{:S(2)}) async-start(), calls=%async_computation.4 | async-start | bytes 524288
  682.4 15.2 %copy-start.11 = (bf16[320,160]{0,1:T(8,128)(2,1)S(1)}, bf16[320,160]{0,1:T(8,128)(2,1)}, u32[]{:S(2)}) copy-start(bf16[320,160]{0,1:T(8,128)(2,1)} %param.15) | copy-start | bytes 307204
Sparse Core Ops, SparseCore 0:
  66.0 203.1 all-reduce.4
  482.1 198.7 all-reduce.6
  698.8 110.1 all-reduce.8
